TPU v7x, 32 devices: a whole 2x2x4 slice. The times are simulated.
32 devices in a mesh: ctx: 16 (over z, y, core), head: 2 (over x).
Axes of the slice: x: 2, y: 2, z: 4, core: 2. Of those that a mesh axis runs over, the one named last changes fastest.
Arguments:
- queries: bfloat16 [2048, 1536], P('ctx', 'head'), may hold values from -45 to 45
- key_rows: bfloat16 [2048, 256], P('ctx', 'head'), may hold values from -5 to 5
- value_rows: bfloat16 [2048, 256], P('ctx', 'head'), may hold values from -18 to 18
- cotangent: bfloat16 [2048, 1536], P('ctx', 'head'), may hold values from -6 to 6
- trace_ids: int32 [2048], P('ctx'), may hold values from 0 to 15, never falling along the last dimension, each value on 1 to 512 neighbouring positions
- correct: int32 [16], replicated, may hold values from 0 to 16, as said below
- group_size: int32 [16], replicated, may hold values from 4 to 16
Outputs:
- log_totals: float32 [2048, 12], P('ctx', 'head')
- grad_queries: float32 [2048, 1536], P('ctx', 'head')
- grad_keys: bfloat16 [2048, 256], P('ctx', 'head')
- grad_values: bfloat16 [2048, 256], P('ctx', 'head')
Inputs may be any that keep to these rules, and one draw needn't show every extreme that they name: correct[g] is at most group_size[g].
All inputs are finite; a program needn't handle non-finite values.
Results may differ from a plain program's by a relative error of at most 0.0054.
Values may be sent and summed in bfloat16 or wider, within the bound.
No kernel may reach another device: no remote copies, remote signals or barrier semaphores. Data moves between devices by JAX's collectives and lax.ppermute only.
A program may use at most 64 MiB of HBM per device.

v0:
```python
import math
import jax
import jax.numpy as jnp
from jax import lax
from jax.sharding import PartitionSpec as P

PASSK = 4


def pass_rate(correct, group_size):
    counts = group_size.astype(jnp.float32)
    hit_counts = correct.astype(jnp.float32)
    product = jnp.ones_like(counts)
    for offset in range(PASSK):
        product = product * (counts - hit_counts - offset) / (counts - offset)
    return 1.0 - product


def body(queries, key_rows, value_rows, cotangent, trace_ids, correct, group_size):
    tok_rows = queries.shape[0]
    half_rows = tok_rows // 2
    row_width = queries.shape[1]
    head_dim = key_rows.shape[1]
    head_count = row_width // head_dim
    ctx_count = lax.axis_size("ctx")
    my_index = lax.axis_index("ctx")
    length = tok_rows * ctx_count
    score_scale = 1.0 / math.sqrt(head_dim)
    pass_rates = pass_rate(correct, group_size)
    traces = jnp.arange(pass_rates.shape[0], dtype=jnp.int32)
    weights = jnp.sum(
        jnp.where(trace_ids[:, None] == traces[None, :], pass_rates[None, :], 0.0), axis=1
    )
    out_grads = (weights[:, None] * cotangent.astype(jnp.float32)).astype(jnp.bfloat16)
    first_base = my_index * tok_rows
    second_base = first_base + half_rows
    local_pos = jnp.arange(half_rows, dtype=jnp.int32)
    positions = jnp.concatenate([first_base + local_pos, second_base + local_pos], 0)
    last_first = first_base + half_rows - 1
    last_second = second_base + half_rows - 1
    query_all = queries.reshape(tok_rows, head_count, head_dim)
    grad_all = out_grads.reshape(tok_rows, head_count, head_dim)

    def run_block(running, key_block, value_block, key_start, block_fn):
        need_first = (key_start <= last_first).astype(jnp.int32)
        need_second = (key_start <= last_second).astype(jnp.int32)
        branch_index = need_first + 2 * need_second

        def skip_block(values_in):
            return values_in

        def first_only(values_in):
            return block_fn((0, half_rows), values_in, key_block, value_block, key_start)

        def second_only(values_in):
            return block_fn((half_rows, tok_rows), values_in, key_block, value_block, key_start)

        def both_halves(values_in):
            return block_fn((0, tok_rows), values_in, key_block, value_block, key_start)

        return lax.switch(branch_index, [skip_block, first_only, second_only, both_halves], running)

    def forward_block(row_span, running, key_block, value_block, key_start):
        row_begin, row_end = row_span
        row_peak, row_total, weighted = running
        query_part = query_all[row_begin:row_end]
        grad_part = grad_all[row_begin:row_end]
        query_pos = positions[row_begin:row_end]
        scores = (
            jnp.einsum("tqd,kd->tqk", query_part, key_block, preferred_element_type=jnp.float32)
            * score_scale
        )
        key_pos = key_start + jnp.arange(key_block.shape[0], dtype=jnp.int32)
        visible = key_pos[None, None, :] <= query_pos[:, None, None]
        block_peak = jnp.max(jnp.where(visible, scores, -1e30), axis=2)
        old_peak = row_peak[row_begin:row_end]
        new_peak = jnp.maximum(old_peak, block_peak)
        exp_terms = jnp.where(visible, jnp.exp(scores - new_peak[:, :, None]), 0.0)
        grad_probs = jnp.einsum(
            "tqd,kd->tqk", grad_part, value_block, preferred_element_type=jnp.float32
        )
        shrink = jnp.exp(old_peak - new_peak)
        new_total = row_total[row_begin:row_end] * shrink + jnp.sum(exp_terms, axis=2)
        new_weighted = weighted[row_begin:row_end] * shrink + jnp.sum(
            exp_terms * grad_probs, axis=2
        )
        return (
            row_peak.at[row_begin:row_end].set(new_peak),
            row_total.at[row_begin:row_end].set(new_total),
            weighted.at[row_begin:row_end].set(new_weighted),
        )

    row_peak = jnp.full((tok_rows, head_count), -1e30, jnp.float32)
    row_total = jnp.zeros((tok_rows, head_count), jnp.float32)
    weighted = jnp.zeros((tok_rows, head_count), jnp.float32)
    key_piece = lax.all_gather(key_rows, "ctx", axis=0, tiled=True)
    value_piece = lax.all_gather(value_rows, "ctx", axis=0, tiled=True)
    piece_rows = key_piece.shape[0]
    block_rows = math.gcd(piece_rows, 512)

    def forward_step(step_index, statistics):
        offset = step_index * block_rows
        key_block = lax.dynamic_slice_in_dim(key_piece, offset, block_rows, 0)
        value_block = lax.dynamic_slice_in_dim(value_piece, offset, block_rows, 0)
        return run_block(statistics, key_block, value_block, offset, forward_block)

    statistics = lax.fori_loop(
        0, piece_rows // block_rows, forward_step, (row_peak, row_total, weighted)
    )
    folded = statistics + (key_piece, value_piece)
    row_peak, row_total, weighted, key_store, value_store = folded
    log_totals = row_peak + jnp.log(row_total)
    delta_rows = weighted / row_total

    def backward_block(row_span, running, key_block, value_block, key_start):
        row_begin, row_end = row_span
        grad_query, zero_block = running
        query_part = query_all[row_begin:row_end]
        grad_part = grad_all[row_begin:row_end]
        query_pos = positions[row_begin:row_end]
        scores = (
            jnp.einsum("tqd,kd->tqk", query_part, key_block, preferred_element_type=jnp.float32)
            * score_scale
        )
        key_pos = key_start + jnp.arange(key_block.shape[0], dtype=jnp.int32)
        visible = key_pos[None, None, :] <= query_pos[:, None, None]
        probabilities = jnp.where(
            visible, jnp.exp(scores - log_totals[row_begin:row_end][:, :, None]), 0.0
        )
        prob_bf16 = probabilities.astype(jnp.bfloat16)
        grad_probs = jnp.einsum(
            "tqd,kd->tqk", grad_part, value_block, preferred_element_type=jnp.float32
        )
        grad_scores = (
            probabilities * (grad_probs - delta_rows[row_begin:row_end][:, :, None])
        ).astype(jnp.bfloat16)
        query_add = (
            jnp.einsum("tqk,kd->tqd", grad_scores, key_block, preferred_element_type=jnp.float32)
            * score_scale
        )
        key_add = (
            jnp.einsum("tqk,tqd->kd", grad_scores, query_part, preferred_element_type=jnp.float32)
            * score_scale
        )
        value_add = jnp.einsum(
            "tqk,tqd->kd", prob_bf16, grad_part, preferred_element_type=jnp.float32
        )
        return (
            grad_query.at[row_begin:row_end].add(query_add),
            jnp.concatenate([key_add, value_add], 1),
        )

    query_zero = jnp.zeros((tok_rows, head_count, head_dim), jnp.float32)
    key_block_rows = math.gcd(length, 512)

    def backward_step(step_index, running):
        grad_query, partial_sums = running
        key_start = step_index * key_block_rows
        key_block = lax.dynamic_slice_in_dim(key_store, key_start, key_block_rows, 0)
        value_block = lax.dynamic_slice_in_dim(value_store, key_start, key_block_rows, 0)
        zero_block = jnp.zeros((key_block_rows, 2 * head_dim), jnp.float32)
        grad_query, block_sums = run_block(
            (grad_query, zero_block), key_block, value_block, key_start, backward_block
        )
        partial_sums = lax.dynamic_update_slice_in_dim(partial_sums, block_sums, key_start, 0)
        return (grad_query, partial_sums)

    grad_query, partial_sums = lax.fori_loop(
        0,
        length // key_block_rows,
        backward_step,
        (query_zero, jnp.zeros((length, 2 * head_dim), jnp.float32)),
    )
    reduced = jnp.sum(
        lax.all_to_all(
            partial_sums.reshape(ctx_count, tok_rows, 2 * head_dim),
            "ctx",
            split_axis=0,
            concat_axis=0,
            tiled=True,
        ),
        axis=0,
    )
    grad_keys = reduced[:, :head_dim].astype(jnp.bfloat16)
    grad_values = reduced[:, head_dim:].astype(jnp.bfloat16)
    query_grads = grad_query.reshape(tok_rows, row_width)
    return (log_totals, query_grads, grad_keys, grad_values)


def solution(mesh):
    return jax.shard_map(
        body,
        mesh=mesh,
        in_specs=(
            P("ctx", "head"),
            P("ctx", "head"),
            P("ctx", "head"),
            P("ctx", "head"),
            P("ctx"),
            P(),
            P(),
        ),
        out_specs=(P("ctx", "head"), P("ctx", "head"), P("ctx", "head"), P("ctx", "head")),
        check_vma=False,
    )
```

profile of v0, /device:TPU:13, one launch (start us, length us, event | category | flops | bytes accessed | tf_op | source)
XLA Modules:
  0.0 124.0 jit_solution(4631487437105801853)
XLA Ops:
  0.7 0.7 fusion.61
  1.4 0.7 select_reduce_fusion.3
  2.1 1.0 multiply_convert_fusion.1
  3.5 1.1 copy.72
  4.8 17.1 %all_gather.6 = bf16[2048,128]{1,0:T(8,128)(2,1)S(1)} all-gather(bf16[128,128]{1,0:T(8,128)(2,1)S(1)} %copy-done.1), channel_id=1, replica_groups=mesh['ctx'=16,'head'=2] {'ctx'}, dimensions={0}, use_global_device_ids=true | all-gather | bytes 557056 | tf_op jit(solution)/shard_map/all_gather | solution.py:96
  21.9 22.8 %all_gather.7 = bf16[2048,128]{1,0:T(8,128)(2,1)S(1)} all-gather(bf16[128,128]{1,0:T(8,128)(2,1)S(1)} %copy-done.2), channel_id=1, replica_groups=mesh['ctx'=16,'head'=2] {'ctx'}, dimensions={0}, use_global_device_ids=true | all-gather | bytes 557056 | tf_op jit(solution)/shard_map/all_gather | solution.py:97
  44.8 3.9 %while.53 = (s32[]{:T(128)}, f32[128,6]{0,1:T(8,128)S(1)}, f32[128,6]{0,1:T(8,128)S(1)}, f32[128,6]{0,1:T(8,128)S(1)}, s32[]{:T(128)}, /*index=5*/s32[]{:T(128)}...) while((s32[]{:T(128)}, f32[128,6]{0,1:T(8,128)S(1)}, ...), condition=%wide.region_15.0_spmd.clone, body=%wide.region_1.15_spmd.clone.sunk | while | flops 205327120 | bytes 6221379 | solution.py:107
  44.8 1.7 %conditional.6 = ((f32[128,6]{0,1:T(8,128)S(1)}, f32[128,6]{0,1:T(8,128)S(1)}, f32[128,6]{0,1:T(8,128)S(1)})) conditional(s32[]{:T(128)} %clamp.18, (f32[128,6]{0,1:T(8,128)S(1)}, f32[128,6]{0,1:T(8,128)S(1)}, f32[128,6]{0,1:T(8,128)S(1)}) %tuple.202, (f32[128,6]{0,1:T(8,128)S(1)}, s32[]{:T(128)}, s32[]{:T(128)}, ...), branch_computations={%region_2.2_spmd, %region_3.6_spmd, %region_7.10_spmd, %region_11.... | conditional | flops 205327104 | bytes 5696036 | solution.py:61
  45.0 0.5 select_reduce_fusion.2
  45.4 0.6 multiply_reduce_fusion
  46.0 0.5 fusion.20
  46.6 1.7 %conditional.6 = ((f32[128,6]{0,1:T(8,128)S(1)}, f32[128,6]{0,1:T(8,128)S(1)}, f32[128,6]{0,1:T(8,128)S(1)})) conditional(s32[]{:T(128)} %clamp.18, (f32[128,6]{0,1:T(8,128)S(1)}, f32[128,6]{0,1:T(8,128)S(1)}, f32[128,6]{0,1:T(8,128)S(1)}) %tuple.202, (f32[128,6]{0,1:T(8,128)S(1)}, s32[]{:T(128)}, s32[]{:T(128)}, ...), branch_computations={%region_2.2_spmd, %region_3.6_spmd, %region_7.10_spmd, %region_11.... | conditional | flops 205327104 | bytes 5696036 | solution.py:61
  46.8 0.5 select_reduce_fusion.2
  47.3 0.6 multiply_reduce_fusion
  47.8 0.5 fusion.20
  48.7 1.5 %broadcast_in_dim.124.clone = f32[2048,256]{1,0:T(8,128)} broadcast(f32[]{:T(128)} %constant.488.clone.1), dimensions={} | broadcast | bytes 2097156 | tf_op jit(solution)/shard_map/broadcast_in_dim | solution.py:172
  50.2 8.7 %while.54 = (s32[]{:T(128)}, f32[128,6,128]{2,0,1:T(8,128)S(1)}, f32[2048,256]{1,0:T(8,128)}, s32[]{:T(128)}, s32[]{:T(128)}, /*index=5*/bf16[2048,128]{1,0:T(8,...) while((s32[]{:T(128)}, f32[128,6,128]{2,0,1:T(8,128)S(1)}, ...), condition=%wide.region_21.22_spmd.clone, body=%wide.region_16.21_spmd.clone.sunk | while | flops 506528256 | bytes 13381159 | solution.py:168
  50.2 2.1 %conditional.7 = (f32[128,6,128]{2,0,1:T(8,128)S(1)}, f32[512,256]{0,1:T(8,128)S(1)}) conditional(s32[]{:T(128)} %clamp.19, f32[128,6,128]{2,0,1:T(8,128)S(1)} %get-tuple-element.1421, (f32[128,6,128]{2,0,1:T(8,128)S(1)}, s32[]{:T(128)}, s32[]{:T(128)}, bf16[128,6,128]{0,2,1:T(8,128)(2,1)S(1)}, ...), branch_computations={%region_17.17_spmd, %region_18.18_spmd, %region_19.19_spmd, %regio... | conditional | flops 506528256 | bytes 10758676 | solution.py:61
  50.4 0.5 exponential_select_fusion.3
  51.2 0.4 multiply_convert_fusion
  52.5 0.8 constant_dynamic-update-slice_fusion.2
  53.4 2.1 %conditional.7 = (f32[128,6,128]{2,0,1:T(8,128)S(1)}, f32[512,256]{0,1:T(8,128)S(1)}) conditional(s32[]{:T(128)} %clamp.19, f32[128,6,128]{2,0,1:T(8,128)S(1)} %get-tuple-element.1421, (f32[128,6,128]{2,0,1:T(8,128)S(1)}, s32[]{:T(128)}, s32[]{:T(128)}, bf16[128,6,128]{0,2,1:T(8,128)(2,1)S(1)}, ...), branch_computations={%region_17.17_spmd, %region_18.18_spmd, %region_19.19_spmd, %regio... | conditional | flops 506528256 | bytes 10758676 | solution.py:61
  53.5 0.5 exponential_select_fusion.3
  55.7 0.9 constant_dynamic-update-slice_fusion.2
  56.9 0.9 constant_dynamic-update-slice_fusion.2
  58.1 0.9 constant_dynamic-update-slice_fusion.2
  58.9 2.9 %copy.78 = f32[16,128,256]{1,2,0:T(8,128)} copy(f32[16,128,256]{2,1,0:T(8,128)} %bitcast.88) | data formatting | bytes 4194304 | tf_op jit(solution)/shard_map/reshape | solution.py:176
  61.8 13.2 %all-to-all-start = ((f32[16,128,256]{1,2,0:T(8,128)}), f32[16,128,256]{1,2,0:T(8,128)S(1)}, u32[]{:S(2)}, u32[]{:S(2)}) async-start(f32[16,128,256]{1,2,0:T(8,128)} %copy.78), calls=%async_computation | async-start | bytes 4194304 | tf_op jit(solution)/shard_map/all_to_all | solution.py:175
  75.2 0.9 copy.80
  76.1 46.3 %all-to-all-done = f32[16,128,256]{1,2,0:T(8,128)S(1)} async-done(((f32[16,128,256]{1,2,0:T(8,128)}), f32[16,128,256]{1,2,0:T(8,128)S(1)}, u32[]{:S(2)}, u32[]{:S(2)}) %all-to-all-start) | async-done | bytes 2097184 | tf_op jit(solution)/shard_map/all_to_all | solution.py:175
  122.5 0.7 copy.82
  123.2 0.7 copy.81
  (76 shorter events, 5.1 us)
Async XLA Ops:
  0.6 4.1 %copy-start.1 = (bf16[128,128]{1,0:T(8,128)(2,1)S(1)}, bf16[128,128]{1,0:T(8,128)(2,1)}, u32[]{:S(2)}) copy-start(bf16[128,128]{1,0:T(8,128)(2,1)} %param.52) | copy-start | bytes 98308
  0.6 21.2 %copy-start.2 = (bf16[128,128]{1,0:T(8,128)(2,1)S(1)}, bf16[128,128]{1,0:T(8,128)(2,1)}, u32[]{:S(2)}) copy-start(bf16[128,128]{1,0:T(8,128)(2,1)} %param.53) | copy-start | bytes 98308
  58.9 2.9 %copy-start = (f32[128,6]{0,1:T(8,128)}, f32[128,6]{0,1:T(8,128)S(1)}, u32[]{:S(2)}) copy-start(f32[128,6]{0,1:T(8,128)S(1)} %get-tuple-element.1469) | copy-start | bytes 9220
  61.8 60.6 %all-to-all-start = ((f32[16,128,256]{1,2,0:T(8,128)}), f32[16,128,256]{1,2,0:T(8,128)S(1)}, u32[]{:S(2)}, u32[]{:S(2)}) async-start(f32[16,128,256]{1,2,0:T(8,128)} %copy.78), calls=%async_computation | async-start | bytes 4194304 | tf_op jit(solution)/shard_map/all_to_all | solution.py:175
where the time goes:
time: 124 us
  waiting for transfers between devices  46.3 us (37%)
  blocking collectives  39.9 us (32%)
  starting transfers between devices  13.2 us (11%)
  local copies, waits for them, and re-layouts  13.1 us (11%)
  matrix products  5.79 us (5%)
  other arithmetic  4.14 us (3%)
    all_to_all x1, waiting for transfers between devices, body(): lax.all_to_all(partial_sums.reshape(ctx_count, tok_rows, 2 * head_dim), '...  46.3 us
    all_gather x1, blocking collectives, body(): value_piece = lax.all_gather(value_rows, 'ctx', axis=0, tiled=True)  22.8 us
    all_gather x1, blocking collectives, body(): key_piece = lax.all_gather(key_rows, 'ctx', axis=0, tiled=True)  17.1 us
    all_to_all x1, starting transfers between devices, body(): lax.all_to_all(partial_sums.reshape(ctx_count, tok_rows, 2 * head_dim), '...  13.2 us
    dynamic_update_slice x8, local copies, waits for them, and re-layouts, backward_step(): lax.dynamic_update_slice_in_dim(partial_sums, block_sums, key_start, 0)  4.17 us
    unnamed x12, local copies, waits for them, and re-layouts  3.83 us
    reshape x1, local copies, waits for them, and re-layouts, body(): partial_sums.reshape(ctx_count, tok_rows, 2 * head_dim)  2.89 us
  transfers between devices with their start and end apart: 1, of which 1 were waited for; matrix products, arithmetic and copies ran while one was open for 1% of the time, Pallas kernels for 0%

commit v1 on v0

--- a/solution.py
+++ b/solution.py
@@ -94,7 +94,14 @@
     row_total = jnp.zeros((tok_rows, head_count), jnp.float32)
     weighted = jnp.zeros((tok_rows, head_count), jnp.float32)
     key_piece = lax.all_gather(key_rows, "ctx", axis=0, tiled=True)
-    value_piece = lax.all_gather(value_rows, "ctx", axis=0, tiled=True)
+    size = lax.axis_size("ctx")
+    right = [(i, (i + 1) % size) for i in range(size)]
+    pieces = [value_rows]
+    for far in range(1, size):
+        pieces = [lax.ppermute(pieces[0], "ctx", right), *pieces]
+    whole = jnp.concatenate(pieces, axis=0)
+    offset_2 = (lax.axis_index("ctx") + 1) * pieces[-1].shape[0]
+    value_piece = jnp.roll(whole, offset_2, axis=0)
     piece_rows = key_piece.shape[0]
     block_rows = math.gcd(piece_rows, 512)
 

time: 124 us -> 181 us (1.46)
  starting transfers between devices: 13.2 us -> 66.6 us
  waiting for transfers between devices: 46.3 us -> 57.9 us
  blocking collectives: 39.9 us -> 31.3 us
    ppermute x0 -> x15, starting transfers between devices: none -> 43.3 us  [body(): pieces = [lax.ppermute(pieces[0], 'ctx', right), *pieces]]
    all_gather x1 -> x0, blocking collectives: 22.8 us -> none  [body(): value_piece = lax.all_gather(value_rows, 'ctx', axis=0, tiled=True)]
    all_gather x1, blocking collectives: 17.1 us -> 31.3 us  [body(): key_piece = lax.all_gather(key_rows, 'ctx', axis=0, tiled=True)]
    ppermute x0 -> x15, waiting for transfers between devices: none -> 11.6 us  [body(): pieces = [lax.ppermute(pieces[0], 'ctx', right), *pieces]]
    all_to_all x1, starting transfers between devices: 13.2 us -> 23.3 us  [body(): lax.all_to_all(partial_sums.reshape(ctx_count, tok_rows, 2 * head_dim), '...]
    unnamed x12 -> x43, local copies, waits for them, and re-layouts: 3.83 us -> 3.2 us
  transfers between devices with their start and end apart: 1 -> 16, of which waited for: 1 -> 14; matrix products, arithmetic and copies ran while one was open for 1% -> 2% of each run, Pallas kernels for 0% -> 0%
where the time goes in v1:
time: 181 us; the launch traced here: 180 us
  starting transfers between devices  66.6 us (37%)
  waiting for transfers between devices  57.9 us (32%)
  blocking collectives  31.3 us (17%)
  local copies, waits for them, and re-layouts  12.5 us (7%)
  matrix products  5.79 us (3%)
  other arithmetic  4.13 us (2%)
    all_to_all x1, waiting for transfers between devices, body(): lax.all_to_all(partial_sums.reshape(ctx_count, tok_rows, 2 * head_dim), '...  46.3 us
    ppermute x15, starting transfers between devices, body(): pieces = [lax.ppermute(pieces[0], 'ctx', right), *pieces]  43.3 us
    all_gather x1, blocking collectives, body(): key_piece = lax.all_gather(key_rows, 'ctx', axis=0, tiled=True)  31.3 us
    all_to_all x1, starting transfers between devices, body(): lax.all_to_all(partial_sums.reshape(ctx_count, tok_rows, 2 * head_dim), '...  23.3 us
    ppermute x15, waiting for transfers between devices, body(): pieces = [lax.ppermute(pieces[0], 'ctx', right), *pieces]  11.6 us
    dynamic_update_slice x8, local copies, waits for them, and re-layouts, backward_step(): lax.dynamic_update_slice_in_dim(partial_sums, block_sums, key_start, 0)  4.13 us
  transfers between devices with their start and end apart: 16, of which 14 were waited for; matrix products, arithmetic and copies ran while one was open for 2% of the time, Pallas kernels for 0%

profile of v1, /device:TPU:13, one launch (start us, length us, event | category | flops | bytes accessed | tf_op | source)
XLA Modules:
  0.0 180.1 jit_solution(12439934738861543800)
XLA Ops:
  0.6 1.9 %collective-permute-start = (bf16[128,128]{1,0:T(8,128)(2,1)}, bf16[128,128]{1,0:T(8,128)(2,1)S(1)}, u32[]{:S(2)}, u32[]{:S(2)}) collective-permute-start(bf16[128,128]{1,0:T(8,128)(2,1)} %param.53), channel_id=1, source_target_pairs={{0,2},{2,4},{4,6},{6,8},{8,10},{10,12},{12,14},{14,16},{16,18},{18... | collective-permute-start | bytes 98312 | tf_op jit(solution)/shard_map/ppermute | solution.py:101
  2.5 1.3 collective-permute-done
  3.8 3.1 %collective-permute-start.1 = (bf16[128,128]{1,0:T(8,128)(2,1)S(1)}, bf16[128,128]{1,0:T(8,128)(2,1)S(1)}, u32[]{:S(2)}, u32[]{:S(2)}) collective-permute-start(bf16[128,128]{1,0:T(8,128)(2,1)S(1)} %collective-permute-done), channel_id=1, source_target_pairs={{0,2},{2,4},{4,6},{6,8},{8,10},{10,12},{12,14},{14,16},{16,18},{18... | collective-permute-start | bytes 98312 | tf_op jit(solution)/shard_map/ppermute | solution.py:101
  6.9 1.0 collective-permute-done.1
  8.0 3.2 %collective-permute-start.2 = (bf16[128,128]{1,0:T(8,128)(2,1)S(1)}, bf16[128,128]{1,0:T(8,128)(2,1)S(1)}, u32[]{:S(2)}, u32[]{:S(2)}) collective-permute-start(bf16[128,128]{1,0:T(8,128)(2,1)S(1)} %collective-permute-done.1), channel_id=1, source_target_pairs={{0,2},{2,4},{4,6},{6,8},{8,10},{10,12},{12,14},{14,16},{16,18},{18... | collective-permute-start | bytes 98312 | tf_op jit(solution)/shard_map/ppermute | solution.py:101
  11.2 1.0 collective-permute-done.2
  12.2 3.2 %collective-permute-start.3 = (bf16[128,128]{1,0:T(8,128)(2,1)S(1)}, bf16[128,128]{1,0:T(8,128)(2,1)S(1)}, u32[]{:S(2)}, u32[]{:S(2)}) collective-permute-start(bf16[128,128]{1,0:T(8,128)(2,1)S(1)} %collective-permute-done.2), channel_id=1, source_target_pairs={{0,2},{2,4},{4,6},{6,8},{8,10},{10,12},{12,14},{14,16},{16,18},{18... | collective-permute-start | bytes 98312 | tf_op jit(solution)/shard_map/ppermute | solution.py:101
  15.4 1.0 collective-permute-done.3
  16.4 3.2 %collective-permute-start.4 = (bf16[128,128]{1,0:T(8,128)(2,1)S(1)}, bf16[128,128]{1,0:T(8,128)(2,1)S(1)}, u32[]{:S(2)}, u32[]{:S(2)}) collective-permute-start(bf16[128,128]{1,0:T(8,128)(2,1)S(1)} %collective-permute-done.3), channel_id=1, source_target_pairs={{0,2},{2,4},{4,6},{6,8},{8,10},{10,12},{12,14},{14,16},{16,18},{18... | collective-permute-start | bytes 98312 | tf_op jit(solution)/shard_map/ppermute | solution.py:101
  19.7 1.0 collective-permute-done.4
  20.7 3.2 %collective-permute-start.5 = (bf16[128,128]{1,0:T(8,128)(2,1)S(1)}, bf16[128,128]{1,0:T(8,128)(2,1)S(1)}, u32[]{:S(2)}, u32[]{:S(2)}) collective-permute-start(bf16[128,128]{1,0:T(8,128)(2,1)S(1)} %collective-permute-done.4), channel_id=1, source_target_pairs={{0,2},{2,4},{4,6},{6,8},{8,10},{10,12},{12,14},{14,16},{16,18},{18... | collective-permute-start | bytes 98312 | tf_op jit(solution)/shard_map/ppermute | solution.py:101
  23.9 1.0 collective-permute-done.5
  24.9 3.2 %collective-permute-start.6 = (bf16[128,128]{1,0:T(8,128)(2,1)S(1)}, bf16[128,128]{1,0:T(8,128)(2,1)S(1)}, u32[]{:S(2)}, u32[]{:S(2)}) collective-permute-start(bf16[128,128]{1,0:T(8,128)(2,1)S(1)} %collective-permute-done.5), channel_id=1, source_target_pairs={{0,2},{2,4},{4,6},{6,8},{8,10},{10,12},{12,14},{14,16},{16,18},{18... | collective-permute-start | bytes 98312 | tf_op jit(solution)/shard_map/ppermute | solution.py:101
  28.1 1.0 collective-permute-done.6
  29.2 3.2 %collective-permute-start.7 = (bf16[128,128]{1,0:T(8,128)(2,1)S(1)}, bf16[128,128]{1,0:T(8,128)(2,1)S(1)}, u32[]{:S(2)}, u32[]{:S(2)}) collective-permute-start(bf16[128,128]{1,0:T(8,128)(2,1)S(1)} %collective-permute-done.6), channel_id=1, source_target_pairs={{0,2},{2,4},{4,6},{6,8},{8,10},{10,12},{12,14},{14,16},{16,18},{18... | collective-permute-start | bytes 98312 | tf_op jit(solution)/shard_map/ppermute | solution.py:101
  33.4 3.2 %collective-permute-start.8 = (bf16[128,128]{1,0:T(8,128)(2,1)S(1)}, bf16[128,128]{1,0:T(8,128)(2,1)S(1)}, u32[]{:S(2)}, u32[]{:S(2)}) collective-permute-start(bf16[128,128]{1,0:T(8,128)(2,1)S(1)} %collective-permute-done.7), channel_id=1, source_target_pairs={{0,2},{2,4},{4,6},{6,8},{8,10},{10,12},{12,14},{14,16},{16,18},{18... | collective-permute-start | bytes 98312 | tf_op jit(solution)/shard_map/ppermute | solution.py:101
  37.6 3.2 %collective-permute-start.9 = (bf16[128,128]{1,0:T(8,128)(2,1)S(1)}, bf16[128,128]{1,0:T(8,128)(2,1)S(1)}, u32[]{:S(2)}, u32[]{:S(2)}) collective-permute-start(bf16[128,128]{1,0:T(8,128)(2,1)S(1)} %collective-permute-done.8), channel_id=1, source_target_pairs={{0,2},{2,4},{4,6},{6,8},{8,10},{10,12},{12,14},{14,16},{16,18},{18... | collective-permute-start | bytes 98312 | tf_op jit(solution)/shard_map/ppermute | solution.py:101
  40.9 31.3 %all_gather.3 = bf16[2048,128]{1,0:T(8,128)(2,1)S(1)} all-gather(bf16[128,128]{1,0:T(8,128)(2,1)} %param.52), channel_id=1, replica_groups=mesh['ctx'=16,'head'=2] {'ctx'}, dimensions={0}, use_global_device_ids=true | all-gather | bytes 557056 | tf_op jit(solution)/shard_map/all_gather | solution.py:96
  73.4 3.0 %collective-permute-start.11 = (bf16[128,128]{1,0:T(8,128)(2,1)S(1)}, bf16[128,128]{1,0:T(8,128)(2,1)S(1)}, u32[]{:S(2)}, u32[]{:S(2)}) collective-permute-start(bf16[128,128]{1,0:T(8,128)(2,1)S(1)} %collective-permute-done.10), channel_id=1, source_target_pairs={{0,2},{2,4},{4,6},{6,8},{8,10},{10,12},{12,14},{14,16},{16,18},{18... | collective-permute-start | bytes 98312 | tf_op jit(solution)/shard_map/ppermute | solution.py:101
  77.5 3.2 %collective-permute-start.12 = (bf16[128,128]{1,0:T(8,128)(2,1)S(1)}, bf16[128,128]{1,0:T(8,128)(2,1)S(1)}, u32[]{:S(2)}, u32[]{:S(2)}) collective-permute-start(bf16[128,128]{1,0:T(8,128)(2,1)S(1)} %collective-permute-done.11), channel_id=1, source_target_pairs={{0,2},{2,4},{4,6},{6,8},{8,10},{10,12},{12,14},{14,16},{16,18},{18... | collective-permute-start | bytes 98312 | tf_op jit(solution)/shard_map/ppermute | solution.py:101
  81.7 3.2 %collective-permute-start.13 = (bf16[128,128]{1,0:T(8,128)(2,1)S(1)}, bf16[128,128]{1,0:T(8,128)(2,1)S(1)}, u32[]{:S(2)}, u32[]{:S(2)}) collective-permute-start(bf16[128,128]{1,0:T(8,128)(2,1)S(1)} %collective-permute-done.12), channel_id=1, source_target_pairs={{0,2},{2,4},{4,6},{6,8},{8,10},{10,12},{12,14},{14,16},{16,18},{18... | collective-permute-start | bytes 98312 | tf_op jit(solution)/shard_map/ppermute | solution.py:101
  86.0 3.2 %collective-permute-start.14 = (bf16[128,128]{1,0:T(8,128)(2,1)S(1)}, bf16[128,128]{1,0:T(8,128)(2,1)S(1)}, u32[]{:S(2)}, u32[]{:S(2)}) collective-permute-start(bf16[128,128]{1,0:T(8,128)(2,1)S(1)} %collective-permute-done.13), channel_id=1, source_target_pairs={{0,2},{2,4},{4,6},{6,8},{8,10},{10,12},{12,14},{14,16},{16,18},{18... | collective-permute-start | bytes 98312 | tf_op jit(solution)/shard_map/ppermute | solution.py:101
  90.8 3.9 %while.53 = (s32[]{:T(128)}, f32[128,6]{0,1:T(8,128)S(1)}, f32[128,6]{0,1:T(8,128)S(1)}, f32[128,6]{0,1:T(8,128)S(1)}, s32[]{:T(128)}, /*index=5*/s32[]{:T(128)}...) while((s32[]{:T(128)}, f32[128,6]{0,1:T(8,128)S(1)}, ...), condition=%wide.region_15.16_spmd.clone, body=%wide.region_1.15_spmd.clone.sunk | while | flops 205327120 | bytes 6221379 | solution.py:114
  90.8 1.7 conditional.6
  92.7 1.7 conditional.6
  94.7 1.5 broadcast_in_dim.124.clone
  96.2 8.7 %while.54 = (s32[]{:T(128)}, f32[128,6,128]{2,0,1:T(8,128)S(1)}, f32[2048,256]{1,0:T(8,128)}, s32[]{:T(128)}, s32[]{:T(128)}, /*index=5*/bf16[2048,128]{1,0:T(8,...) while((s32[]{:T(128)}, f32[128,6,128]{2,0,1:T(8,128)S(1)}, ...), condition=%wide.region_21.22_spmd.clone, body=%wide.region_16.21_spmd.clone.sunk | while | flops 506528256 | bytes 13381159 | solution.py:175
  96.2 2.1 %conditional.7 = (f32[128,6,128]{2,0,1:T(8,128)S(1)}, f32[512,256]{0,1:T(8,128)S(1)}) conditional(s32[]{:T(128)} %clamp.19, f32[128,6,128]{2,0,1:T(8,128)S(1)} %get-tuple-element.1421, (f32[128,6,128]{2,0,1:T(8,128)S(1)}, s32[]{:T(128)}, s32[]{:T(128)}, bf16[128,6,128]{0,2,1:T(8,128)(2,1)S(1)}, ...), branch_computations={%region_17.17_spmd, %region_18.18_spmd, %region_19.19_spmd, %regio... | conditional | flops 506528256 | bytes 10758676 | solution.py:61
  99.4 2.1 %conditional.7 = (f32[128,6,128]{2,0,1:T(8,128)S(1)}, f32[512,256]{0,1:T(8,128)S(1)}) conditional(s32[]{:T(128)} %clamp.19, f32[128,6,128]{2,0,1:T(8,128)S(1)} %get-tuple-element.1421, (f32[128,6,128]{2,0,1:T(8,128)S(1)}, s32[]{:T(128)}, s32[]{:T(128)}, bf16[128,6,128]{0,2,1:T(8,128)(2,1)S(1)}, ...), branch_computations={%region_17.17_spmd, %region_18.18_spmd, %region_19.19_spmd, %regio... | conditional | flops 506528256 | bytes 10758676 | solution.py:61
  104.9 2.9 %copy.78 = f32[16,128,256]{1,2,0:T(8,128)} copy(f32[16,128,256]{2,1,0:T(8,128)} %bitcast.88) | data formatting | bytes 4194304 | tf_op jit(solution)/shard_map/reshape | solution.py:183
  107.8 23.3 %all-to-all-start = ((f32[16,128,256]{1,2,0:T(8,128)}), f32[16,128,256]{1,2,0:T(8,128)S(1)}, u32[]{:S(2)}, u32[]{:S(2)}) async-start(f32[16,128,256]{1,2,0:T(8,128)} %copy.78), calls=%async_computation | async-start | bytes 4194304 | tf_op jit(solution)/shard_map/all_to_all | solution.py:182
  132.2 46.3 %all-to-all-done = f32[16,128,256]{1,2,0:T(8,128)S(1)} async-done(((f32[16,128,256]{1,2,0:T(8,128)}), f32[16,128,256]{1,2,0:T(8,128)S(1)}, u32[]{:S(2)}, u32[]{:S(2)}) %all-to-all-start) | async-done | bytes 2097184 | tf_op jit(solution)/shard_map/all_to_all | solution.py:182
  (138 shorter events, 22.4 us)
Async XLA Ops:
  0.6 89.0 %copy-start = (bf16[128,768]{1,0:T(8,128)(2,1)S(1)}, bf16[128,768]{1,0:T(8,128)(2,1)}, u32[]{:S(2)}) copy-start(bf16[128,768]{1,0:T(8,128)(2,1)} %param.51) | copy-start | bytes 589828
  0.6 3.2 %collective-permute-start = (bf16[128,128]{1,0:T(8,128)(2,1)}, bf16[128,128]{1,0:T(8,128)(2,1)S(1)}, u32[]{:S(2)}, u32[]{:S(2)}) collective-permute-start(bf16[128,128]{1,0:T(8,128)(2,1)} %param.53), channel_id=1, source_target_pairs={{0,2},{2,4},{4,6},{6,8},{8,10},{10,12},{12,14},{14,16},{16,18},{18... | collective-permute-start | bytes 98312 | tf_op jit(solution)/shard_map/ppermute | solution.py:101
  3.8 4.1 %collective-permute-start.1 = (bf16[128,128]{1,0:T(8,128)(2,1)S(1)}, bf16[128,128]{1,0:T(8,128)(2,1)S(1)}, u32[]{:S(2)}, u32[]{:S(2)}) collective-permute-start(bf16[128,128]{1,0:T(8,128)(2,1)S(1)} %collective-permute-done), channel_id=1, source_target_pairs={{0,2},{2,4},{4,6},{6,8},{8,10},{10,12},{12,14},{14,16},{16,18},{18... | collective-permute-start | bytes 98312 | tf_op jit(solution)/shard_map/ppermute | solution.py:101
  8.0 4.2 %collective-permute-start.2 = (bf16[128,128]{1,0:T(8,128)(2,1)S(1)}, bf16[128,128]{1,0:T(8,128)(2,1)S(1)}, u32[]{:S(2)}, u32[]{:S(2)}) collective-permute-start(bf16[128,128]{1,0:T(8,128)(2,1)S(1)} %collective-permute-done.1), channel_id=1, source_target_pairs={{0,2},{2,4},{4,6},{6,8},{8,10},{10,12},{12,14},{14,16},{16,18},{18... | collective-permute-start | bytes 98312 | tf_op jit(solution)/shard_map/ppermute | solution.py:101
  12.2 4.2 %collective-permute-start.3 = (bf16[128,128]{1,0:T(8,128)(2,1)S(1)}, bf16[128,128]{1,0:T(8,128)(2,1)S(1)}, u32[]{:S(2)}, u32[]{:S(2)}) collective-permute-start(bf16[128,128]{1,0:T(8,128)(2,1)S(1)} %collective-permute-done.2), channel_id=1, source_target_pairs={{0,2},{2,4},{4,6},{6,8},{8,10},{10,12},{12,14},{14,16},{16,18},{18... | collective-permute-start | bytes 98312 | tf_op jit(solution)/shard_map/ppermute | solution.py:101
  16.4 4.2 %collective-permute-start.4 = (bf16[128,128]{1,0:T(8,128)(2,1)S(1)}, bf16[128,128]{1,0:T(8,128)(2,1)S(1)}, u32[]{:S(2)}, u32[]{:S(2)}) collective-permute-start(bf16[128,128]{1,0:T(8,128)(2,1)S(1)} %collective-permute-done.3), channel_id=1, source_target_pairs={{0,2},{2,4},{4,6},{6,8},{8,10},{10,12},{12,14},{14,16},{16,18},{18... | collective-permute-start | bytes 98312 | tf_op jit(solution)/shard_map/ppermute | solution.py:101
  20.7 4.2 %collective-permute-start.5 = (bf16[128,128]{1,0:T(8,128)(2,1)S(1)}, bf16[128,128]{1,0:T(8,128)(2,1)S(1)}, u32[]{:S(2)}, u32[]{:S(2)}) collective-permute-start(bf16[128,128]{1,0:T(8,128)(2,1)S(1)} %collective-permute-done.4), channel_id=1, source_target_pairs={{0,2},{2,4},{4,6},{6,8},{8,10},{10,12},{12,14},{14,16},{16,18},{18... | collective-permute-start | bytes 98312 | tf_op jit(solution)/shard_map/ppermute | solution.py:101
  24.9 4.2 %collective-permute-start.6 = (bf16[128,128]{1,0:T(8,128)(2,1)S(1)}, bf16[128,128]{1,0:T(8,128)(2,1)S(1)}, u32[]{:S(2)}, u32[]{:S(2)}) collective-permute-start(bf16[128,128]{1,0:T(8,128)(2,1)S(1)} %collective-permute-done.5), channel_id=1, source_target_pairs={{0,2},{2,4},{4,6},{6,8},{8,10},{10,12},{12,14},{14,16},{16,18},{18... | collective-permute-start | bytes 98312 | tf_op jit(solution)/shard_map/ppermute | solution.py:101
  29.2 4.2 %collective-permute-start.7 = (bf16[128,128]{1,0:T(8,128)(2,1)S(1)}, bf16[128,128]{1,0:T(8,128)(2,1)S(1)}, u32[]{:S(2)}, u32[]{:S(2)}) collective-permute-start(bf16[128,128]{1,0:T(8,128)(2,1)S(1)} %collective-permute-done.6), channel_id=1, source_target_pairs={{0,2},{2,4},{4,6},{6,8},{8,10},{10,12},{12,14},{14,16},{16,18},{18... | collective-permute-start | bytes 98312 | tf_op jit(solution)/shard_map/ppermute | solution.py:101
  33.4 4.2 %collective-permute-start.8 = (bf16[128,128]{1,0:T(8,128)(2,1)S(1)}, bf16[128,128]{1,0:T(8,128)(2,1)S(1)}, u32[]{:S(2)}, u32[]{:S(2)}) collective-permute-start(bf16[128,128]{1,0:T(8,128)(2,1)S(1)} %collective-permute-done.7), channel_id=1, source_target_pairs={{0,2},{2,4},{4,6},{6,8},{8,10},{10,12},{12,14},{14,16},{16,18},{18... | collective-permute-start | bytes 98312 | tf_op jit(solution)/shard_map/ppermute | solution.py:101
  37.6 34.6 %collective-permute-start.9 = (bf16[128,128]{1,0:T(8,128)(2,1)S(1)}, bf16[128,128]{1,0:T(8,128)(2,1)S(1)}, u32[]{:S(2)}, u32[]{:S(2)}) collective-permute-start(bf16[128,128]{1,0:T(8,128)(2,1)S(1)} %collective-permute-done.8), channel_id=1, source_target_pairs={{0,2},{2,4},{4,6},{6,8},{8,10},{10,12},{12,14},{14,16},{16,18},{18... | collective-permute-start | bytes 98312 | tf_op jit(solution)/shard_map/ppermute | solution.py:101
  72.2 18.2 %copy-start.2 = (bf16[128,128]{1,0:T(8,128)(2,1)S(1)}, bf16[128,128]{1,0:T(8,128)(2,1)}, u32[]{:S(2)}) copy-start(bf16[128,128]{1,0:T(8,128)(2,1)} %param.53) | copy-start | bytes 98308
  72.2 1.2 collective-permute-start.10
  73.4 4.1 %collective-permute-start.11 = (bf16[128,128]{1,0:T(8,128)(2,1)S(1)}, bf16[128,128]{1,0:T(8,128)(2,1)S(1)}, u32[]{:S(2)}, u32[]{:S(2)}) collective-permute-start(bf16[128,128]{1,0:T(8,128)(2,1)S(1)} %collective-permute-done.10), channel_id=1, source_target_pairs={{0,2},{2,4},{4,6},{6,8},{8,10},{10,12},{12,14},{14,16},{16,18},{18... | collective-permute-start | bytes 98312 | tf_op jit(solution)/shard_map/ppermute | solution.py:101
  77.5 4.3 %collective-permute-start.12 = (bf16[128,128]{1,0:T(8,128)(2,1)S(1)}, bf16[128,128]{1,0:T(8,128)(2,1)S(1)}, u32[]{:S(2)}, u32[]{:S(2)}) collective-permute-start(bf16[128,128]{1,0:T(8,128)(2,1)S(1)} %collective-permute-done.11), channel_id=1, source_target_pairs={{0,2},{2,4},{4,6},{6,8},{8,10},{10,12},{12,14},{14,16},{16,18},{18... | collective-permute-start | bytes 98312 | tf_op jit(solution)/shard_map/ppermute | solution.py:101
  81.7 4.2 %collective-permute-start.13 = (bf16[128,128]{1,0:T(8,128)(2,1)S(1)}, bf16[128,128]{1,0:T(8,128)(2,1)S(1)}, u32[]{:S(2)}, u32[]{:S(2)}) collective-permute-start(bf16[128,128]{1,0:T(8,128)(2,1)S(1)} %collective-permute-done.12), channel_id=1, source_target_pairs={{0,2},{2,4},{4,6},{6,8},{8,10},{10,12},{12,14},{14,16},{16,18},{18... | collective-permute-start | bytes 98312 | tf_op jit(solution)/shard_map/ppermute | solution.py:101
  86.0 4.2 %collective-permute-start.14 = (bf16[128,128]{1,0:T(8,128)(2,1)S(1)}, bf16[128,128]{1,0:T(8,128)(2,1)S(1)}, u32[]{:S(2)}, u32[]{:S(2)}) collective-permute-start(bf16[128,128]{1,0:T(8,128)(2,1)S(1)} %collective-permute-done.13), channel_id=1, source_target_pairs={{0,2},{2,4},{4,6},{6,8},{8,10},{10,12},{12,14},{14,16},{16,18},{18... | collective-permute-start | bytes 98312 | tf_op jit(solution)/shard_map/ppermute | solution.py:101
  104.9 2.9 %copy-start.1 = (f32[128,6]{0,1:T(8,128)}, f32[128,6]{0,1:T(8,128)S(1)}, u32[]{:S(2)}) copy-start(f32[128,6]{0,1:T(8,128)S(1)} %get-tuple-element.1469) | copy-start | bytes 9220
  107.8 70.7 %all-to-all-start = ((f32[16,128,256]{1,2,0:T(8,128)}), f32[16,128,256]{1,2,0:T(8,128)S(1)}, u32[]{:S(2)}, u32[]{:S(2)}) async-start(f32[16,128,256]{1,2,0:T(8,128)} %copy.78), calls=%async_computation | async-start | bytes 4194304 | tf_op jit(solution)/shard_map/all_to_all | solution.py:182
